TPU v7x, 32 devices: a whole 2x2x4 slice. The times are simulated.
32 devices in a mesh: groups: 2 (over x), tensor: 16 (over z, y, core).
Axes of the slice: x: 2, y: 2, z: 4, core: 2. Of those that a mesh axis runs over, the one named last changes fastest.
Arguments:
- tokens: bfloat16 [256, 8192], P(('groups', 'tensor')), parts along dimension 0, may hold values from -6 to 6
- gate_weight: bfloat16 [8192, 28672], P(None, 'tensor'), may hold values from -0.0625 to 0.0625
- up_weight: bfloat16 [8192, 28672], P(None, 'tensor'), may hold values from -0.0625 to 0.0625
- adapter_down_weight: bfloat16 [16, 8192, 64], P('tensor'), may hold values from -0.0625 to 0.0625
- adapter_up_weight: bfloat16 [16, 64, 28672], P(None, None, 'tensor'), may hold values from -0.75 to 0.75
- token_adapter_index: int32 [256, 1], P(('groups', 'tensor')), parts along dimension 0, may hold values from 0 to 15; in each aligned block of 128 rows (0 to 127, 128 to 255, ...) at most 16 rows name the same one
- adapter_slot_index: int32 [16], replicated, may hold values from 0 to 15, each once
Outputs:
- hidden: bfloat16 [256, 28672], P('groups', 'tensor'), parts along dimension 0
There are 2 independent parts, one for each index of `groups`. A program takes and returns all parts, laid end to end along the dimension named above; an argument that names none is the same for every part. Nothing has to cross between parts.
Inputs may be any that keep to these rules, and one draw needn't show every extreme that they name: `token_adapter_index`: in every draw at most 16 of all 128 tokens use one adapter, and some adapter is used by exactly 16 tokens; every adapter is used by some token. `adapter_slot_index`: A permutation; slot s is stored on the device of index s along tensor.
All inputs are finite; a program needn't handle non-finite values.
Results may differ from a plain program's by a relative error of at most 0.0039.
Values may be sent and summed in bfloat16 or wider, within the bound.
No kernel may reach another device: no remote copies, remote signals or barrier semaphores. Data moves between devices by JAX's collectives and lax.ppermute only.
A program may use at most 192 MiB of HBM per device.

v0:
```python
import math
import jax
import jax.numpy as jnp
from jax import lax
from jax.sharding import PartitionSpec as P


def body(
    tokens,
    gate_weight,
    up_weight,
    adapter_down_weight,
    adapter_up_weight,
    token_adapter_index,
    adapter_slot_index,
):
    me = lax.axis_index("tensor")
    hidden_per_device = gate_weight.shape[1]
    all_ids = lax.all_gather(token_adapter_index, "tensor", axis=0, tiled=True)[:, 0]
    total = all_ids.shape[0]
    resident_weight = adapter_slot_index.shape[0]
    table_hits = all_ids[:, None] == jnp.arange(resident_weight, dtype=jnp.int32)[None, :]
    slot_of = jnp.sum(jnp.where(table_hits, adapter_slot_index[None, :], 0), axis=1)
    local_portion = lax.all_gather(tokens, "tensor", axis=0, tiled=True)
    mine = slot_of == me
    reduced_input = jnp.dot(
        local_portion, adapter_down_weight[0], preferred_element_type=jnp.float32
    )
    reduced_input = jnp.where(mine[:, None], reduced_input, 0.0)
    products = jnp.concatenate(
        [
            jnp.dot(local_portion, gate_weight, preferred_element_type=jnp.float32),
            jnp.dot(local_portion, up_weight, preferred_element_type=jnp.float32),
            reduced_input,
        ],
        axis=1,
    )
    gate = products[:, :hidden_per_device]
    up = products[:, hidden_per_device : 2 * hidden_per_device]
    low_part = products[:, 2 * hidden_per_device :]
    adapter_delta = lax.psum(low_part, "tensor").astype(jnp.bfloat16)
    device_position = adapter_delta.shape[1]
    up_weight_slice = adapter_up_weight.reshape(
        resident_weight * device_position, hidden_per_device
    )
    block = math.gcd(total, 256)
    low_blocks = adapter_delta.reshape(total // block, block, device_position)
    slot_blocks = slot_of.reshape(total // block, block)
    slot_range = jnp.arange(resident_weight, dtype=jnp.int32)

    def lift(args):
        reduced_input, selected_slot = args
        hits = selected_slot[:, None, None] == slot_range[None, :, None]
        spread = jnp.where(hits, reduced_input[:, None, :], jnp.zeros((), jnp.bfloat16)).reshape(
            reduced_input.shape[0], resident_weight * device_position
        )
        return jnp.dot(spread, up_weight_slice, preferred_element_type=jnp.float32)

    delta = lax.map(lift, (low_blocks, slot_blocks)).reshape(total, hidden_per_device)
    return (jax.nn.silu(gate) * (up + delta)).astype(jnp.bfloat16)


def solution(mesh):
    in_specs = (
        P(("groups", "tensor"), None),
        P(None, "tensor"),
        P(None, "tensor"),
        P("tensor", None, None),
        P(None, None, "tensor"),
        P(("groups", "tensor"), None),
        P(),
    )
    out_specs = P("groups", "tensor")
    return jax.shard_map(body, mesh=mesh, in_specs=in_specs, out_specs=out_specs, check_vma=False)
```

profile of v0, /device:TPU:0, one launch (start us, length us, event | category | flops | bytes accessed | tf_op | source)
XLA Modules:
  0.0 151.4 jit_solution(16022517166369663602)
XLA Ops:
  6.5 0.0 copy-start
  6.5 0.0 all-gather.2.cloned.1.call-start
  6.5 0.7 all-gather.2.cloned.1.call-update
  7.3 1.2 dynamic-slice.2
  9.2 0.8 bitcast_dynamic-update-slice_fusion
  9.9 13.8 %all-reduce = s32[128]{0:T(128)S(1)} all-reduce(s32[128]{0:T(128)S(1)} %bitcast_dynamic-update-slice_fusion), channel_id=1, replica_groups=mesh['groups'=2,'tensor'=16] {'tensor'}, use_global_device_ids=true, to_apply=%add | all-reduce | flops 128 | bytes 1024
  23.7 0.7 select_reduce_fusion
  24.5 29.1 %all-gather.2.cloned.1.call-done = bf16[128,8192]{1,0:T(8,128)(2,1)} async-done(((bf16[8,8192]{1,0:T(8,128)(2,1)}), bf16[128,8192]{1,0:T(8,128)(2,1)}) %all-gather.2.cloned.1.call-update) | async-done | bytes 2097168 | tf_op jit(solution)/shard_map/all_gather | solution.py:24
  53.7 0.0 copy-done
  53.7 0.0 copy-start.2
  53.7 2.6 %convolution_select_fusion = f32[128,64]{0,1:T(8,128)S(1)} fusion(bf16[128,8192]{1,0:T(8,128)(2,1)} %all-gather.2.cloned.1.call-done, bf16[1,8192,64]{1,2,0:T(8,128)(2,1)S(1)} %copy-done, pred[128]{0:T(512)(128)(4,1)S(1)} %broadcast_compare_fusion), kind=kOutput, calls=%fused_computation.4 | convolution fusion | flops 134225920 | bytes 3178624 | tf_op jit(solution)/shard_map/dot_general | solution.py:26
  56.2 59.5 %psum.7 = bf16[128,64]{0,1:T(8,128)(2,1)S(1)} all-reduce(f32[128,64]{0,1:T(8,128)S(1)} %convolution_select_fusion), channel_id=1, replica_groups=mesh['groups'=2,'tensor'=16] {'tensor'}, use_global_device_ids=true, to_apply=%region_1.2 | all-reduce | flops 8192 | bytes 49152 | tf_op jit(solution)/shard_map/psum | solution.py:41
  115.7 2.7 %convolution_bitcast_fusion = f32[128,1792]{1,0:T(8,128)S(1)} fusion(bf16[16,64,1792]{2,1,0:T(8,128)(2,1)} %param.11, pred[128,16]{0,1:T(8,128)(4,1)S(1)} %iota_compare_fusion, bf16[128,64]{0,1:T(8,128)(2,1)S(1)} %psum.7), kind=kOutput, calls=%fused_computation | convolution fusion | flops 469893120 | bytes 4605952 | tf_op jit(solution)/shard_map/while/body/eval_jaxpr/dot_general | solution.py:57
  118.4 0.0 copy-done.2
  118.4 11.7 %fusion.8 = f32[128,1792]{1,0:T(8,128)S(1)} fusion(bf16[128,8192]{1,0:T(8,128)(2,1)S(1)} %copy-done.2, bf16[8192,1792]{1,0:T(8,128)(2,1)} %param.8), kind=kOutput, calls=%fused_computation.16 | convolution fusion | flops 3758096384 | bytes 32374784 | tf_op jit(solution)/shard_map/dot_general | solution.py:32
  130.2 0.0 copy-start.1
  130.2 14.4 %fusion.1 = bf16[128,1792]{1,0:T(8,128)(2,1)} fusion(f32[128,1792]{1,0:T(8,128)S(1)} %convolution_bitcast_fusion, bf16[128,8192]{1,0:T(8,128)(2,1)S(1)} %copy-done.2, bf16[8192,1792]{1,0:T(8,128)(2,1)} %param.9, f32[128,1792]{1,0:T(8,128)S(1)} %fusion.8), kind=kOutput, calls=%fused_computation.3 | convolution fusion | flops 3759702016 | bytes 33751040 | tf_op jit(solution)/shard_map/dot_general | solution.py:33
  144.5 0.0 copy-done.1
  (3 shorter events, 0.0 us)
Async XLA Ops:
  6.5 47.1 %copy-start = (bf16[1,8192,64]{1,2,0:T(8,128)(2,1)S(1)}, bf16[1,8192,64]{1,2,0:T(8,128)(2,1)}, u32[]{:S(2)}) copy-start(bf16[1,8192,64]{1,2,0:T(8,128)(2,1)} %param.10) | copy-start | bytes 3145732
  6.5 47.1 %all-gather.2.cloned.1.call-start = ((), (), s32[]{:S(2)}) async-start(), calls=%async_computation | async-start | bytes 2228224 | tf_op jit(solution)/shard_map/all_gather | solution.py:24
  53.7 64.8 %copy-start.2 = (bf16[128,8192]{1,0:T(8,128)(2,1)S(1)}, bf16[128,8192]{1,0:T(8,128)(2,1)}, u32[]{:S(2)}) copy-start(bf16[128,8192]{1,0:T(8,128)(2,1)} %all-gather.2.cloned.1.call-done) | copy-start | bytes 6291460
  130.2 14.4 %copy-start.1 = (bf16[1,8192,64]{1,2,0:T(8,128)(2,1)S(1)}, bf16[1,8192,64]{1,2,0:T(8,128)(2,1)}, u32[]{:S(2)}) copy-start(bf16[1,8192,64]{1,2,0:T(8,128)(2,1)} %param.10) | copy-start | bytes 3145732
Sparse Core Ops, SparseCore 0:
  9.5 44.0 all-gather.1
where the time goes:
time: 152 us; the launch traced here: 151 us
  blocking collectives  73.3 us (48%)
  matrix products  31.4 us (21%)
  waiting for transfers between devices  29.9 us (20%)
  between operations  14.1 us (9%)
  local copies, waits for them, and re-layouts  2.01 us (1%)
    psum x1, blocking collectives, body(): adapter_delta = lax.psum(low_part, 'tensor').astype(jnp.bfloat16)  59.5 us
    all_gather x1, waiting for transfers between devices, body(): local_portion = lax.all_gather(tokens, 'tensor', axis=0, tiled=True)  29.1 us
    dot_general x1, matrix products, body(): jnp.dot(local_portion, up_weight, preferred_element_type=jnp.float32)  14.4 us
    unnamed x1, blocking collectives  13.8 us
    dot_general x1, matrix products, body(): jnp.dot(local_portion, gate_weight, preferred_element_type=jnp.float32)  11.7 us
  transfers between devices with their start and end apart: 1, of which 1 were waited for; matrix products, arithmetic and copies ran while one was open for 2% of the time, Pallas kernels for 0%

commit v1 on v0

--- a/solution.py
+++ b/solution.py
@@ -3,6 +3,12 @@
 import jax.numpy as jnp
 from jax import lax
 from jax.sharding import PartitionSpec as P
+
+
+def summed_here(x, mesh_axis):
+    shards = lax.all_gather(x, mesh_axis, axis=0, tiled=False)
+    result = shards.sum(axis=0)
+    return result
 
 
 def body(
@@ -38,7 +44,7 @@
     gate = products[:, :hidden_per_device]
     up = products[:, hidden_per_device : 2 * hidden_per_device]
     low_part = products[:, 2 * hidden_per_device :]
-    adapter_delta = lax.psum(low_part, "tensor").astype(jnp.bfloat16)
+    adapter_delta = summed_here(low_part, "tensor").astype(jnp.bfloat16)
     device_position = adapter_delta.shape[1]
     up_weight_slice = adapter_up_weight.reshape(
         resident_weight * device_position, hidden_per_device

time: 152 us -> 111 us (0.73)
  blocking collectives: 73.3 us -> 34.6 us
  matrix products: 31.4 us -> 29.3 us
    psum x1 -> x0, blocking collectives: 59.5 us -> none  [body(): adapter_delta = lax.psum(low_part, 'tensor').astype(jnp.bfloat16)]
    all_gather x0 -> x1, blocking collectives: none -> 20.7 us  [summed_here(): shards = lax.all_gather(x, mesh_axis, axis=0, tiled=False)]
    dot_general x1, matrix products: 2.71 us -> 0.67 us  [lift(): return jnp.dot(spread, up_weight_slice, preferred_element_type=jnp.float32)]
where the time goes in v1:
time: 111 us
  blocking collectives  34.6 us (31%)
  waiting for transfers between devices  29.9 us (27%)
  matrix products  29.3 us (26%)
  between operations  14.1 us (13%)
  local copies, waits for them, and re-layouts  2.11 us (2%)
    all_gather x1, waiting for transfers between devices, body(): local_portion = lax.all_gather(tokens, 'tensor', axis=0, tiled=True)  29.1 us
    all_gather x1, blocking collectives, summed_here(): shards = lax.all_gather(x, mesh_axis, axis=0, tiled=False)  20.7 us
    dot_general x1, matrix products, body(): jnp.dot(local_portion, up_weight, preferred_element_type=jnp.float32)  14.4 us
    unnamed x1, blocking collectives  13.8 us
    dot_general x1, matrix products, body(): jnp.dot(local_portion, gate_weight, preferred_element_type=jnp.float32)  11.7 us
    dot_general x1, matrix products, body(): jnp.dot(local_portion, adapter_down_weight[0], preferred_element_type=jnp...  2.58 us
  transfers between devices with their start and end apart: 1, of which 1 were waited for; matrix products, arithmetic and copies ran while one was open for 2% of the time, Pallas kernels for 0%

profile of v1, /device:TPU:0, one launch (start us, length us, event | category | flops | bytes accessed | tf_op | source)
XLA Modules:
  0.0 110.9 jit_solution(9689183251922081512)
XLA Ops:
  6.5 0.0 copy-start
  6.5 0.0 all-gather.3.cloned.1.call-start
  6.5 0.7 all-gather.3.cloned.1.call-update
  7.3 1.2 %dynamic-slice.2 = u32[1]{0:T(128)} dynamic-slice(u32[32]{0:T(128)} %constant.30, u32[]{:T(128)S(6)} %add.11), dynamic_slice_sizes={1} | dynamic-slice | bytes 12
  9.2 0.8 bitcast_dynamic-update-slice_fusion
  9.9 13.8 %all-reduce = s32[128]{0:T(128)S(1)} all-reduce(s32[128]{0:T(128)S(1)} %bitcast_dynamic-update-slice_fusion), channel_id=1, replica_groups=mesh['groups'=2,'tensor'=16] {'tensor'}, use_global_device_ids=true, to_apply=%add | all-reduce | flops 128 | bytes 1024
  23.7 0.7 select_reduce_fusion
  24.5 29.1 %all-gather.3.cloned.1.call-done = bf16[128,8192]{1,0:T(8,128)(2,1)} async-done(((bf16[8,8192]{1,0:T(8,128)(2,1)}), bf16[128,8192]{1,0:T(8,128)(2,1)}) %all-gather.3.cloned.1.call-update) | async-done | bytes 2097168 | tf_op jit(solution)/shard_map/all_gather | solution.py:30
  53.7 0.0 copy-done
  53.7 0.0 copy-start.3
  53.7 2.6 %convolution_select_fusion = f32[128,64]{0,1:T(8,128)S(1)} fusion(bf16[128,8192]{1,0:T(8,128)(2,1)} %all-gather.3.cloned.1.call-done, bf16[1,8192,64]{1,2,0:T(8,128)(2,1)S(1)} %copy-done, pred[128]{0:T(512)(128)(4,1)S(1)} %broadcast_compare_fusion), kind=kOutput, calls=%fused_computation.4 | convolution fusion | flops 134225920 | bytes 3178624 | tf_op jit(solution)/shard_map/dot_general | solution.py:32
  56.2 0.0 copy-start.2
  56.3 20.7 %all-gather = f32[2048,64]{0,1:T(8,128)S(1)} all-gather(f32[128,64]{0,1:T(8,128)S(1)} %convolution_select_fusion), channel_id=2, replica_groups=mesh['groups'=2,'tensor'=16] {'tensor'}, dimensions={0}, use_global_device_ids=true | all-gather | bytes 557056 | tf_op jit(solution)/shard_map/all_gather | solution.py:9
  77.0 0.1 copy.8
  77.1 0.1 bitcast_reduce_fusion
  77.2 0.0 copy-done.3
  77.2 0.7 convolution_bitcast_fusion
  77.9 0.0 copy-done.2
  77.9 11.7 %fusion.8 = f32[128,1792]{1,0:T(8,128)S(1)} fusion(bf16[128,8192]{1,0:T(8,128)(2,1)S(1)} %copy-done.2, bf16[8192,1792]{1,0:T(8,128)(2,1)} %param.8), kind=kOutput, calls=%fused_computation.17 | convolution fusion | flops 3758096384 | bytes 32374784 | tf_op jit(solution)/shard_map/dot_general | solution.py:38
  89.6 0.0 copy-start.1
  89.6 14.4 %fusion.1 = bf16[128,1792]{1,0:T(8,128)(2,1)} fusion(f32[128,1792]{1,0:T(8,128)S(1)} %convolution_bitcast_fusion, bf16[128,8192]{1,0:T(8,128)(2,1)S(1)} %copy-done.2, bf16[8192,1792]{1,0:T(8,128)(2,1)} %param.9, f32[128,1792]{1,0:T(8,128)S(1)} %fusion.8), kind=kOutput, calls=%fused_computation.3 | convolution fusion | flops 3759702016 | bytes 33751040 | tf_op jit(solution)/shard_map/dot_general | solution.py:39
  104.0 0.0 copy-done.1
  (3 shorter events, 0.0 us)
Async XLA Ops:
  6.5 47.1 %copy-start = (bf16[1,8192,64]{1,2,0:T(8,128)(2,1)S(1)}, bf16[1,8192,64]{1,2,0:T(8,128)(2,1)}, u32[]{:S(2)}) copy-start(bf16[1,8192,64]{1,2,0:T(8,128)(2,1)} %param.10) | copy-start | bytes 3145732
  6.5 47.1 %all-gather.3.cloned.1.call-start = ((), (), s32[]{:S(2)}) async-start(), calls=%async_computation | async-start | bytes 2228224 | tf_op jit(solution)/shard_map/all_gather | solution.py:30
  53.7 23.5 %copy-start.3 = (bf16[16,64,1792]{2,1,0:T(8,128)(2,1)S(1)}, bf16[16,64,1792]{2,1,0:T(8,128)(2,1)}, u32[]{:S(2)}) copy-start(bf16[16,64,1792]{2,1,0:T(8,128)(2,1)} %param.11) | copy-start | bytes 11010052
  56.2 21.6 %copy-start.2 = (bf16[128,8192]{1,0:T(8,128)(2,1)S(1)}, bf16[128,8192]{1,0:T(8,128)(2,1)}, u32[]{:S(2)}) copy-start(bf16[128,8192]{1,0:T(8,128)(2,1)} %all-gather.3.cloned.1.call-done) | copy-start | bytes 6291460
  89.6 14.4 %copy-start.1 = (bf16[1,8192,64]{1,2,0:T(8,128)(2,1)S(1)}, bf16[1,8192,64]{1,2,0:T(8,128)(2,1)}, u32[]{:S(2)}) copy-start(bf16[1,8192,64]{1,2,0:T(8,128)(2,1)} %param.10) | copy-start | bytes 3145732
Sparse Core Ops, SparseCore 0:
  9.5 44.0 all-gather.2
